TPU v7x, 32 devices: a whole 2x2x4 slice. The times are simulated.
32 devices in a mesh: attn: 8 (over z, y), exp: 4 (over x, core).
Axes of the slice: x: 2, y: 2, z: 4, core: 2. Of those that a mesh axis runs over, the one named last changes fastest.
Arguments:
- q_latent: bfloat16 [16, 128, 512], P('attn'), may hold values from -6 to 6
- q_rope: bfloat16 [16, 64, 128], P('attn'), may hold values from -8 to 8
- cache_latent: bfloat16 [16, 4096, 512], P('attn', 'exp'), may hold values from -6 to 6
- cache_rope: bfloat16 [16, 64, 4096], P('attn', None, 'exp'), may hold values from -8 to 8
- lengths: int32 [16], P('attn'), may hold values from 2 to 4096, as said below
- tokens: bfloat16 [256, 7168], P(('attn', 'exp')), may hold values from -6 to 6
- route_ids: int32 [256, 4], P(('attn', 'exp')), may hold values from 0 to 7, all different within a row; in each aligned block of 8 rows (0 to 7, 8 to 15, ...) at most 8 rows name the same one
- route_gates: float32 [256, 4], P(('attn', 'exp')), may hold values from 0.2 to 1
- w_gate: bfloat16 [8, 7168, 1024], P('attn', None, 'exp'), may hold values from -0.0625 to 0.0625
- w_up: bfloat16 [8, 7168, 1024], P('attn', None, 'exp'), may hold values from -0.0625 to 0.0625
- w_down: bfloat16 [8, 1024, 7168], P('attn', 'exp'), may hold values from -0.1875 to 0.1875
Outputs:
- attn_out: bfloat16 [16, 128, 512], P('attn', 'exp')
- moe_out: bfloat16 [256, 7168], P(('attn', 'exp'))
Inputs may be any that keep to these rules, and one draw needn't show every extreme that they name: `route_ids`: within the rows of one device (aligned blocks of 8 rows) an expert is named at most 8 times; a token names 4 distinct experts. `lengths`: some request has length exactly 4096.
All inputs are finite; a program needn't handle non-finite values.
Results may differ from a plain program's by a relative error of at most 0.0058.
Values may be sent and summed in bfloat16 or wider, within the bound.
No kernel may reach another device: no remote copies, remote signals or barrier semaphores. Data moves between devices by JAX's collectives and lax.ppermute only.
A program may use at most 128 MiB of HBM per device.

v0:
```python
import math
import jax
import jax.numpy as jnp
from jax import lax
from jax.sharding import PartitionSpec as P

score_scale = 1.0 / math.sqrt(192.0)
neg_fill = -1e30


def expert_part(row_block, gate_slice, up_slice, down_slice):
    gate_value = jnp.dot(row_block, gate_slice, preferred_element_type=jnp.float32)
    upward = jnp.dot(row_block, up_slice, preferred_element_type=jnp.float32)
    hidden = (jax.nn.silu(gate_value) * upward).astype(jnp.bfloat16)
    return jnp.dot(hidden, down_slice, preferred_element_type=jnp.float32)


def per_device(
    q_latent,
    q_rope,
    cache_latent,
    cache_rope,
    lengths,
    tokens,
    route_ids,
    route_gates,
    w_gate,
    w_up,
    w_down,
):
    n_exp = lax.axis_size("exp")
    n_attn = lax.axis_size("attn")
    positions = cache_latent.shape[1]
    scores = jnp.einsum("rhl,rpl->rhp", q_latent, cache_latent, preferred_element_type=jnp.float32)
    scores = scores + jnp.einsum(
        "rdh,rdp->rhp", q_rope, cache_rope, preferred_element_type=jnp.float32
    )
    scores = score_scale * scores
    global_pos = lax.axis_index("exp") * positions + jnp.arange(positions, dtype=jnp.int32)
    is_live = global_pos[None, None, :] < lengths[:, None, None]
    masked = jnp.where(is_live, scores, neg_fill)
    block_max = jnp.max(masked, axis=2)
    weights = jnp.where(is_live, jnp.exp(masked - block_max[:, :, None]), 0.0)
    block_sum = jnp.sum(weights, axis=2)
    block_out = jnp.einsum(
        "rhp,rpl->rhl",
        weights.astype(jnp.bfloat16),
        cache_latent,
        preferred_element_type=jnp.float32,
    )
    row_top = lax.pmax(block_max, "exp")
    factor = jnp.exp(block_max - row_top)
    numerator, denominator = (
        lax.psum_scatter(block_out * factor[:, :, None], "exp", scatter_dimension=1, tiled=True),
        lax.psum_scatter(block_sum * factor, "exp", scatter_dimension=1, tiled=True),
    )
    attn_out = (numerator / denominator[:, :, None]).astype(jnp.bfloat16)
    n_local = w_gate.shape[0]
    all_axes = ("attn", "exp")
    tok_all = lax.all_gather(tokens, all_axes, axis=0, tiled=True)
    ids_all = lax.all_gather(route_ids, all_axes, axis=0, tiled=True)
    gates_all = lax.all_gather(route_gates, all_axes, axis=0, tiled=True)
    first_expert = lax.axis_index("attn") * n_local
    partial = None
    for i in range(n_local):
        weight = jnp.sum(jnp.where(ids_all == first_expert + i, gates_all, 0.0), axis=1)
        piece = expert_part(tok_all, w_gate[i], w_up[i], w_down[i]) * weight[:, None]
        partial = piece if partial is None else partial + piece
    moe_out = lax.psum_scatter(partial, all_axes, scatter_dimension=0, tiled=True).astype(
        jnp.bfloat16
    )
    return (attn_out, moe_out)


def solution(mesh):
    return jax.shard_map(
        per_device,
        mesh=mesh,
        in_specs=(
            P("attn", None, None),
            P("attn", None, None),
            P("attn", "exp", None),
            P("attn", None, "exp"),
            P("attn"),
            P(("attn", "exp"), None),
            P(("attn", "exp"), None),
            P(("attn", "exp"), None),
            P("attn", None, "exp"),
            P("attn", None, "exp"),
            P("attn", "exp", None),
        ),
        out_specs=(P("attn", "exp", None), P(("attn", "exp"), None)),
        check_vma=False,
    )
```

profile of v0, /device:TPU:0, one launch (start us, length us, event | category | flops | bytes accessed | tf_op | source)
XLA Modules:
  0.0 270.4 jit_solution(11026204819615197221)
XLA Ops:
  8.0 0.0 copy-start
  8.0 0.0 copy-start.1
  8.0 0.0 all-gather.4.cloned.1.call-start
  8.1 0.7 all-gather.4.cloned.1.call-update
  8.8 0.0 reduce-scatter.10.cloned.1.call-start
  8.8 0.7 broadcast_compare_fusion
  9.6 0.0 copy-done
  9.6 1.8 fusion.31
  11.4 0.0 copy-done.1
  11.4 0.0 copy-start.2
  11.4 0.0 copy-start.3
  11.4 1.2 fusion.30
  12.6 8.3 %pmax.7 = f32[2,128]{1,0:T(2,128)S(1)} all-reduce(f32[2,128]{1,0:T(2,128)S(1)} %get-tuple-element.4), channel_id=1, replica_groups=mesh['attn'=8,'exp'=4] {'exp'}, use_global_device_ids=true, to_apply=%region_1.2 | all-reduce | flops 256 | bytes 2048 | tf_op jit(solution)/shard_map/pmax | solution.py:51
  20.9 0.3 fusion.15
  21.3 0.7 copy.13
  22.0 0.0 reduce-scatter.10.cloned.1.call-update
  22.0 0.0 reduce-scatter.6.cloned.1.call-start
  22.1 1.4 convolution_multiply_fusion.1
  23.5 0.0 reduce-scatter.6.cloned.1.call-update
  23.5 0.0 reduce-scatter.8.cloned.1.call-start
  23.5 0.0 copy-done.2
  23.6 41.1 %all-gather = s32[32,8,4]{1,2,0:T(4,128)S(1)} all-gather(s32[1,8,4]{1,2,0:T(4,128)S(1)} %bitcast.28), channel_id=1, replica_groups=mesh['attn'=8,'exp'=4] {'attn','exp'}, dimensions={0}, use_global_device_ids=true | all-gather | bytes 4224 | tf_op jit(solution)/shard_map/all_gather | solution.py:61
  64.6 0.0 copy-done.3
  64.7 36.8 %all-gather.1 = f32[32,8,4]{1,2,0:T(4,128)S(1)} all-gather(f32[1,8,4]{1,2,0:T(4,128)S(1)} %bitcast.29), channel_id=1, replica_groups=mesh['attn'=8,'exp'=4] {'attn','exp'}, dimensions={0}, use_global_device_ids=true | all-gather | bytes 4224 | tf_op jit(solution)/shard_map/all_gather | solution.py:62
  101.5 0.1 select_reduce_fusion
  101.5 0.1 reshape.49
  101.6 0.0 all-gather.4.cloned.1.call-done
  101.6 4.3 %fusion.3 = f32[256,256]{1,0:T(8,128)S(1)} fusion(bf16[256,7168]{1,0:T(8,128)(2,1)} %all-gather.4.cloned.1.call-done, bf16[1,7168,256]{2,1,0:T(8,128)(2,1)} %param.19), kind=kOutput, calls=%fused_computation.4 | convolution fusion | flops 939524096 | bytes 7602176 | tf_op jit(solution)/shard_map/dot_general | solution.py:12
  105.9 11.2 %convolution_multiply_fusion = f32[256,7168]{1,0:T(8,128)} fusion(bf16[1,256,7168]{2,1,0:T(8,128)(2,1)} %param.21, f32[256]{0:T(256)S(1)} %reshape.49, bf16[256,7168]{1,0:T(8,128)(2,1)} %all-gather.4.cloned.1.call-done, bf16[1,7168,256]{2,1,0:T(8,128)(2,1)} %param.20, f32[256,256]{1,0:T(8,128)S(1)} %fusion.3), kind=kOutput, calls=%fused_computation | convolution fusion | flops 1881276416 | bytes 18613248 | tf_op jit(solution)/shard_map/dot_general | solution.py:15
  117.1 0.0 reduce-scatter.8.cloned.1.call-update
  117.1 0.0 reduce-scatter.10.cloned.1.call-done
  117.1 0.8 copy.14
  117.9 0.0 reduce-scatter.6.cloned.1.call-done
  117.9 1.6 divide_convert_fusion
  119.6 141.6 %reduce-scatter.8.cloned.1.call-done = f32[8,7168]{1,0:T(8,128)} async-done(((f32[256,7168]{1,0:T(8,128)}), f32[8,7168]{1,0:T(8,128)}) %reduce-scatter.8.cloned.1.call-update) | async-done | bytes 229392 | tf_op jit(solution)/shard_map/reduce_scatter | solution.py:69
  261.2 1.6 convert_element_type.15
  (2 shorter events, 0.0 us)
Async XLA Ops:
  8.0 1.6 copy-start
  8.0 3.3 %copy-start.1 = (bf16[2,64,1024]{2,1,0:T(8,128)(2,1)S(1)}, bf16[2,64,1024]{2,1,0:T(8,128)(2,1)}, u32[]{:S(2)}) copy-start(bf16[2,64,1024]{2,1,0:T(8,128)(2,1)} %param.14) | copy-start | bytes 786436
  8.0 93.6 %all-gather.4.cloned.1.call-start = ((), (), s32[]{:S(2)}) async-start(), calls=%async_computation.4 | async-start | bytes 3784704 | tf_op jit(solution)/shard_map/all_gather | solution.py:60
  8.8 108.4 %reduce-scatter.10.cloned.1.call-start = ((), (), s32[]{:S(2)}) async-start(), calls=%async_computation.6 | async-start | bytes 81920
  11.4 12.2 %copy-start.2 = (s32[8,4]{0,1:T(4,128)S(1)}, s32[8,4]{0,1:T(4,128)}, u32[]{:S(2)}) copy-start(s32[8,4]{0,1:T(4,128)} %param.17) | copy-start | bytes 388
  11.4 53.3 %copy-start.3 = (f32[8,4]{0,1:T(4,128)S(1)}, f32[8,4]{0,1:T(4,128)}, u32[]{:S(2)}) copy-start(f32[8,4]{0,1:T(4,128)} %param.18) | copy-start | bytes 388
  22.0 95.9 %reduce-scatter.6.cloned.1.call-start = ((), (), s32[]{:S(2)}) async-start(), calls=%async_computation.3 | async-start | bytes 655360 | tf_op jit(solution)/shard_map/reduce_scatter | solution.py:54
  23.5 237.7 %reduce-scatter.8.cloned.1.call-start = ((), (), s32[]{:S(2)}) async-start(), calls=%async_computation.5 | async-start | bytes 7569408 | tf_op jit(solution)/shard_map/reduce_scatter | solution.py:69
Sparse Core Ops, SparseCore 0:
  11.7 63.1 all-gather.3
Sparse Core Ops, SparseCore 1:
  22.1 19.7 reduce-scatter.9
  44.4 25.2 reduce-scatter.5
  117.2 144.0 reduce-scatter.7
where the time goes:
time: 271 us; the launch traced here: 270 us
  waiting for transfers between devices  142 us (52%)
  blocking collectives  86.2 us (32%)
  matrix products  19.8 us (7%)
  between operations  15.8 us (6%)
  other arithmetic  4.34 us (2%)
    reduce_scatter x1, waiting for transfers between devices, per_device(): lax.psum_scatter(partial, all_axes, scatter_dimension=0, tiled=True)  142 us
    all_gather x1, blocking collectives, per_device(): ids_all = lax.all_gather(route_ids, all_axes, axis=0, tiled=True)  41.1 us
    all_gather x1, blocking collectives, per_device(): gates_all = lax.all_gather(route_gates, all_axes, axis=0, tiled=True)  36.8 us
    dot_general x1, matrix products, expert_part(): return jnp.dot(hidden, down_slice, preferred_element_type=jnp.float32)  11.2 us
    pmax x1, blocking collectives, per_device(): row_top = lax.pmax(block_max, 'exp')  8.33 us
  transfers between devices with their start and end apart: 4, of which 1 were waited for; matrix products, arithmetic and copies ran while one was open for 9% of the time, Pallas kernels for 0%

commit v1 on v0

--- a/solution.py
+++ b/solution.py
@@ -58,8 +58,13 @@
     n_local = w_gate.shape[0]
     all_axes = ("attn", "exp")
     tok_all = lax.all_gather(tokens, all_axes, axis=0, tiled=True)
-    ids_all = lax.all_gather(route_ids, all_axes, axis=0, tiled=True)
-    gates_all = lax.all_gather(route_gates, all_axes, axis=0, tiled=True)
+    ids_all, gates_all = jnp.split(
+        lax.all_gather(
+            jnp.concatenate([route_ids, route_gates], 1), axis_name=all_axes, axis=0, tiled=True
+        ),
+        [route_ids.shape[1]],
+        1,
+    )
     first_expert = lax.axis_index("attn") * n_local
     partial = None
     for i in range(n_local):

time: 271 us -> 246 us (0.908)
  blocking collectives: 86.2 us -> 49.6 us
  waiting for transfers between devices: 142 us -> 154 us
    all_gather x2 -> x1, blocking collectives: 77.9 us -> 41.3 us  [per_device(): lax.all_gather(jnp.concatenate([route_ids, route_gates], 1), axis_name=al...]
    all_gather x1, waiting for transfers between devices: 0.02 us -> 9.63 us  [per_device(): tok_all = lax.all_gather(tokens, all_axes, axis=0, tiled=True)]
  transfers between devices with their start and end apart: 4 -> 4, of which waited for: 1 -> 2; matrix products, arithmetic and copies ran while one was open for 9% -> 10% of each run, Pallas kernels for 0% -> 0%
where the time goes in v1:
time: 246 us; the launch traced here: 245 us
  waiting for transfers between devices  154 us (63%)
  blocking collectives  49.6 us (20%)
  matrix products  19.8 us (8%)
  between operations  15.8 us (6%)
  other arithmetic  4.55 us (2%)
    reduce_scatter x1, waiting for transfers between devices, per_device(): lax.psum_scatter(partial, all_axes, scatter_dimension=0, tiled=True)  143 us
    all_gather x1, blocking collectives, per_device(): lax.all_gather(jnp.concatenate([route_ids, route_gates], 1), axis_name=al...  41.3 us
    dot_general x1, matrix products, expert_part(): return jnp.dot(hidden, down_slice, preferred_element_type=jnp.float32)  11.2 us
    all_gather x1, waiting for transfers between devices, per_device(): tok_all = lax.all_gather(tokens, all_axes, axis=0, tiled=True)  9.63 us
    pmax x1, blocking collectives, per_device(): row_top = lax.pmax(block_max, 'exp')  8.33 us
  transfers between devices with their start and end apart: 4, of which 2 were waited for; matrix products, arithmetic and copies ran while one was open for 10% of the time, Pallas kernels for 0%

profile of v1, /device:TPU:0, one launch (start us, length us, event | category | flops | bytes accessed | tf_op | source)
XLA Modules:
  0.0 245.1 jit_solution(15644179566429213008)
XLA Ops:
  8.0 0.0 copy-start
  8.0 0.0 copy-start.1
  8.0 0.0 all-gather.2.cloned.1.call-start
  8.1 0.7 all-gather.2.cloned.1.call-update
  8.8 0.0 reduce-scatter.10.cloned.1.call-start
  8.8 0.7 broadcast_compare_fusion
  9.6 0.0 copy-done
  9.6 1.8 fusion.32
  11.4 0.0 copy-done.1
  11.4 0.0 copy-start.2
  11.4 0.0 copy-start.3
  11.4 1.2 fusion.31
  12.6 8.3 %pmax.7 = f32[2,128]{1,0:T(2,128)S(1)} all-reduce(f32[2,128]{1,0:T(2,128)S(1)} %get-tuple-element.4), channel_id=1, replica_groups=mesh['attn'=8,'exp'=4] {'exp'}, use_global_device_ids=true, to_apply=%region_1.2 | all-reduce | flops 256 | bytes 2048 | tf_op jit(solution)/shard_map/pmax | solution.py:51
  20.9 0.3 fusion.15
  21.3 0.7 copy.15
  22.0 0.0 reduce-scatter.10.cloned.1.call-update
  22.0 0.0 reduce-scatter.6.cloned.1.call-start
  22.1 1.4 convolution_multiply_fusion.1
  23.5 0.0 reduce-scatter.6.cloned.1.call-update
  23.5 0.0 reduce-scatter.8.cloned.1.call-start
  23.5 0.0 copy-done.2
  23.6 0.1 copy.13
  23.6 0.0 copy-done.3
  23.6 0.1 copy.14
  23.7 0.1 pad_maximum_fusion
  23.8 41.3 %all_gather.7 = f32[256,8]{1,0:T(8,128)S(1)} all-gather(f32[8,8]{1,0:T(8,128)S(1)} %pad_maximum_fusion), channel_id=1, replica_groups=mesh['attn'=8,'exp'=4] {'attn','exp'}, dimensions={0}, use_global_device_ids=true | all-gather | bytes 8448 | tf_op jit(solution)/shard_map/all_gather | solution.py:62
  65.1 0.2 fusion.26
  65.3 9.6 %all-gather.2.cloned.1.call-done = bf16[256,7168]{1,0:T(8,128)(2,1)} async-done(((bf16[8,7168]{1,0:T(8,128)(2,1)}), bf16[256,7168]{1,0:T(8,128)(2,1)}) %all-gather.2.cloned.1.call-update) | async-done | bytes 3670032 | tf_op jit(solution)/shard_map/all_gather | solution.py:60
  74.9 4.3 %fusion.3 = f32[256,256]{1,0:T(8,128)S(1)} fusion(bf16[256,7168]{1,0:T(8,128)(2,1)} %all-gather.2.cloned.1.call-done, bf16[1,7168,256]{2,1,0:T(8,128)(2,1)} %param.19), kind=kOutput, calls=%fused_computation.4 | convolution fusion | flops 939524096 | bytes 7602176 | tf_op jit(solution)/shard_map/dot_general | solution.py:12
  79.2 11.2 %convolution_multiply_fusion = f32[256,7168]{1,0:T(8,128)} fusion(bf16[1,256,7168]{2,1,0:T(8,128)(2,1)} %param.21, f32[256]{0:T(256)S(1)} %fusion.26, bf16[256,7168]{1,0:T(8,128)(2,1)} %all-gather.2.cloned.1.call-done, bf16[1,7168,256]{2,1,0:T(8,128)(2,1)} %param.20, f32[256,256]{1,0:T(8,128)S(1)} %fusion.3), kind=kOutput, calls=%fused_computation | convolution fusion | flops 1881276416 | bytes 18613248 | tf_op jit(solution)/shard_map/dot_general | solution.py:15
  90.4 0.0 reduce-scatter.8.cloned.1.call-update
  90.4 0.0 reduce-scatter.10.cloned.1.call-done
  90.4 0.8 copy.16
  91.2 0.0 reduce-scatter.6.cloned.1.call-done
  91.2 1.6 divide_convert_fusion
  92.8 143.1 %reduce-scatter.8.cloned.1.call-done = f32[8,7168]{1,0:T(8,128)} async-done(((f32[256,7168]{1,0:T(8,128)}), f32[8,7168]{1,0:T(8,128)}) %reduce-scatter.8.cloned.1.call-update) | async-done | bytes 229392 | tf_op jit(solution)/shard_map/reduce_scatter | solution.py:74
  236.0 1.6 convert_element_type.23
  (3 shorter events, 0.0 us)
Async XLA Ops:
  8.0 1.6 copy-start
  8.0 3.3 %copy-start.1 = (bf16[2,64,1024]{2,1,0:T(8,128)(2,1)S(1)}, bf16[2,64,1024]{2,1,0:T(8,128)(2,1)}, u32[]{:S(2)}) copy-start(bf16[2,64,1024]{2,1,0:T(8,128)(2,1)} %param.14) | copy-start | bytes 786436
  8.0 66.9 %all-gather.2.cloned.1.call-start = ((), (), s32[]{:S(2)}) async-start(), calls=%async_computation.4 | async-start | bytes 3784704 | tf_op jit(solution)/shard_map/all_gather | solution.py:60
  8.8 81.6 %reduce-scatter.10.cloned.1.call-start = ((), (), s32[]{:S(2)}) async-start(), calls=%async_computation.6 | async-start | bytes 81920
  11.4 12.2 %copy-start.2 = (s32[8,4]{0,1:T(4,128)S(1)}, s32[8,4]{0,1:T(4,128)}, u32[]{:S(2)}) copy-start(s32[8,4]{0,1:T(4,128)} %param.17) | copy-start | bytes 388
  11.4 12.3 %copy-start.3 = (f32[8,4]{0,1:T(4,128)S(1)}, f32[8,4]{0,1:T(4,128)}, u32[]{:S(2)}) copy-start(f32[8,4]{0,1:T(4,128)} %param.18) | copy-start | bytes 388
  22.0 69.2 %reduce-scatter.6.cloned.1.call-start = ((), (), s32[]{:S(2)}) async-start(), calls=%async_computation.3 | async-start | bytes 655360 | tf_op jit(solution)/shard_map/reduce_scatter | solution.py:54
  23.5 212.5 %reduce-scatter.8.cloned.1.call-start = ((), (), s32[]{:S(2)}) async-start(), calls=%async_computation.5 | async-start | bytes 7569408 | tf_op jit(solution)/shard_map/reduce_scatter | solution.py:74
Sparse Core Ops, SparseCore 0:
  11.7 63.1 all-gather.1
Sparse Core Ops, SparseCore 1:
  22.1 19.7 reduce-scatter.9
  44.4 25.2 reduce-scatter.5
  90.5 145.4 reduce-scatter.7
